TPU v7x, 128 devices: a whole 4x4x4 slice. The times are simulated.
128 devices in a mesh: dp: 32 (over z, y, core), mp: 4 (over x).
Axes of the slice: x: 4, y: 4, z: 4, core: 2. Of those that a mesh axis runs over, the one named last changes fastest.
Arguments:
- tokens: bfloat16 [57344, 1024], P('dp'), may hold values from -60 to 60
- segment_ids: int32 [57344], P('dp'), may hold values from 0 to 127, as said below
- page_table: int32 [448], P('dp'), may hold values from 0 to 447, as said below
- w_query: bfloat16 [1024, 1024], P('dp', 'mp'), may hold values from -0.1875 to 0.1875
- w_key: bfloat16 [1024, 1024], P('dp', 'mp'), may hold values from -0.1875 to 0.1875
- w_value: bfloat16 [1024, 1024], P('dp', 'mp'), may hold values from -0.1875 to 0.1875
- w_out: bfloat16 [1024, 1024], P('mp', 'dp'), may hold values from -1.5 to 1.5
- w_up: bfloat16 [1024, 4096], P('dp', 'mp'), may hold values from -0.1875 to 0.1875
- w_down: bfloat16 [4096, 1024], P('mp', 'dp'), may hold values from -0.09375 to 0.09375
- gain_first: float32 [1024], replicated, may hold values from 0.1 to 1.9
- shift_first: float32 [1024], replicated, may hold values from -3 to 3
- gain_second: float32 [1024], replicated, may hold values from 0.1 to 1.9
- shift_second: float32 [1024], replicated, may hold values from -3 to 3
Outputs:
- mixed: bfloat16 [57344, 1024], P('dp')
- kv_cache: bfloat16 [57344, 2, 1024], P('dp', None, 'mp')
Inputs may be any that keep to these rules, and one draw needn't show every extreme that they name: page_table is a permutation of the page slots. Page p lies on device p // 14 in arrival order and goes to device page_table[p] // 14; from one device at most 1 pages go to one device, and some pair reaches 1. `segment_ids`: tokens with equal ids form one request; after dealing, a request's tokens are consecutive and lie on one device, which holds at most 4 requests.
All inputs are finite; a program needn't handle non-finite values.
Results may differ from a plain program's by a relative error of at most 0.014.
Values may be sent and summed in bfloat16 or wider, within the bound.
No kernel may reach another device: no remote copies, remote signals or barrier semaphores. Data moves between devices by JAX's collectives and lax.ppermute only.
A program may use at most 128 MiB of HBM per device.

v0:
```python
import jax
import jax.numpy as jnp
from jax import lax
from jax.sharding import PartitionSpec as P

HEAD = 64


def layer_norm(hidden_sum, gain, shift):
    center = hidden_sum - jnp.mean(hidden_sum, axis=-1, keepdims=True)
    spread = jnp.mean(center * center, axis=-1, keepdims=True)
    return center * lax.rsqrt(spread + 1e-05) * gain + shift


def attend_head(query, keys, values, segments, block_rows):
    blocks = query.shape[0] // block_rows
    query_blocks = query.reshape(blocks, block_rows, query.shape[1])
    segment_blocks = segments.reshape(blocks, block_rows)

    def per_block(bundle):
        rows, row_ids = bundle
        scores = jnp.einsum("qd,kd->qk", rows, keys, preferred_element_type=jnp.float32) * HEAD ** (
            -0.5
        )
        scores = jnp.where(row_ids[:, None] == segments[None, :], scores, -1e30)
        highest = jnp.max(scores, axis=1, keepdims=True)
        raised = jnp.exp(scores - highest)
        attn_weights = (raised / jnp.sum(raised, axis=1, keepdims=True)).astype(jnp.bfloat16)
        return jnp.dot(attn_weights, values, preferred_element_type=jnp.float32).astype(
            jnp.bfloat16
        )

    return lax.map(per_block, (query_blocks, segment_blocks)).reshape(
        query.shape[0], values.shape[1]
    )


def finish(partial_value, residual, gain, shift):
    total = lax.psum(partial_value.astype(jnp.bfloat16), "mp").astype(jnp.float32)
    return layer_norm(residual.astype(jnp.float32) + total, gain, shift).astype(jnp.bfloat16)


def outgoing_pages(source, got_slots, pages_dev, page):
    paged = source.reshape(pages_dev, page, source.shape[1])[jnp.clip(got_slots, 0, pages_dev - 1)]
    return jnp.where((got_slots >= 0)[:, None, None], paged, jnp.zeros_like(paged))


def body(
    tokens,
    segment_ids,
    page_table,
    w_query,
    w_key,
    w_value,
    w_out,
    w_up,
    w_down,
    gain_first,
    shift_first,
    gain_second,
    shift_second,
):
    n_data = lax.axis_size("dp")
    pages_dev = page_table.shape[0]
    page = tokens.shape[0] // pages_dev
    width = tokens.shape[1]
    slots_per = (pages_dev + n_data - 1) // n_data
    buffer_rows = n_data * slots_per
    target = page_table // pages_dev
    local_slot = page_table % pages_dev
    order = jnp.arange(pages_dev, dtype=jnp.int32)
    earlier = (target[:, None] == target[None, :]) & (order[:, None] < order[None, :])
    rank = jnp.sum(earlier.astype(jnp.int32), axis=0)
    position = target * slots_per + rank
    send_ids = (
        jnp.zeros((buffer_rows, page), jnp.int32)
        .at[position]
        .set(segment_ids.reshape(pages_dev, page))
    )
    send_slots = jnp.full((buffer_rows,), -1, jnp.int32).at[position].set(local_slot)
    send_pages = (
        jnp.zeros((buffer_rows, page, width), tokens.dtype)
        .at[position]
        .set(tokens.reshape(pages_dev, page, width))
    )
    got_pages, got_ids, got_slots = (
        lax.all_to_all(send_pages, "dp", split_axis=0, concat_axis=0, tiled=True),
        lax.all_to_all(send_ids, "dp", split_axis=0, concat_axis=0, tiled=True),
        lax.all_to_all(send_slots, "dp", split_axis=0, concat_axis=0, tiled=True),
    )
    matches = got_slots[None, :] == order[:, None]
    source_row = jnp.sum(
        jnp.where(matches, jnp.arange(buffer_rows, dtype=jnp.int32)[None, :], 0), axis=1
    )
    dealt = got_pages[source_row].reshape(pages_dev * page, got_pages.shape[2])
    dealt_ids = got_ids[source_row].reshape(pages_dev * page)
    full_query, full_key, full_value, full_up, full_out, full_down = (
        lax.all_gather(w_query, "dp", axis=0, tiled=True),
        lax.all_gather(w_key, "dp", axis=0, tiled=True),
        lax.all_gather(w_value, "dp", axis=0, tiled=True),
        lax.all_gather(w_up, "dp", axis=0, tiled=True),
        lax.all_gather(w_out, "dp", axis=1, tiled=True),
        lax.all_gather(w_down, "dp", axis=1, tiled=True),
    )
    query = jnp.dot(dealt, full_query, preferred_element_type=jnp.float32).astype(jnp.bfloat16)
    keys = jnp.dot(dealt, full_key, preferred_element_type=jnp.float32).astype(jnp.bfloat16)
    values = jnp.dot(dealt, full_value, preferred_element_type=jnp.float32).astype(jnp.bfloat16)
    suitable = [
        count for count in range(1, pages_dev + 1) if pages_dev % count == 0 and count * page >= 512
    ]
    block_rows = suitable[0] * page
    heads_here = query.shape[1] // HEAD
    contexts = []
    for head in range(heads_here):
        cols = slice(head * HEAD, (head + 1) * HEAD)
        contexts.append(
            attend_head(query[:, cols], keys[:, cols], values[:, cols], dealt_ids, block_rows)
        )
    context = jnp.concatenate(contexts, axis=1)
    partial_value = jnp.dot(context, full_out, preferred_element_type=jnp.float32)
    first = finish(partial_value, dealt, gain_first, shift_first)
    hidden = jax.nn.gelu(
        jnp.dot(first, full_up, preferred_element_type=jnp.float32), approximate=False
    ).astype(jnp.bfloat16)
    second = finish(
        jnp.dot(hidden, full_down, preferred_element_type=jnp.float32),
        first,
        gain_second,
        shift_second,
    )
    returned = lax.all_to_all(
        outgoing_pages(second, got_slots, pages_dev, page),
        "dp",
        split_axis=0,
        concat_axis=0,
        tiled=True,
    )
    mixed = returned[position].reshape(pages_dev * page, width)
    kv_cache = jnp.stack([keys, values], axis=1)
    return (mixed, kv_cache)


def solution(mesh):
    return jax.shard_map(
        body,
        mesh=mesh,
        in_specs=(
            P("dp", None),
            P("dp"),
            P("dp"),
            P("dp", "mp"),
            P("dp", "mp"),
            P("dp", "mp"),
            P("mp", "dp"),
            P("dp", "mp"),
            P("mp", "dp"),
            P(),
            P(),
            P(),
            P(),
        ),
        out_specs=(P("dp", None), P("dp", None, "mp")),
        check_vma=False,
    )
```

profile of v0, /device:TPU:0, one launch (start us, length us, event | category | flops | bytes accessed | tf_op | source)
XLA Modules:
  0.0 663.7 jit_solution(7760421901178392480)
XLA Ops:
  10.1 8.4 %all-to-all-start = ((s32[32,1,1]{2,1,0:T(1,128)}), s32[32,1,1]{2,1,0:T(1,128)S(1)}, u32[]{:S(2)}, u32[]{:S(2)}) async-start(s32[32,1,1]{2,1,0:T(1,128)} %copy.81), calls=%async_computation | async-start | bytes 32768 | tf_op jit(solution)/shard_map/all_to_all | solution.py:89
  19.8 6.1 all-to-all-done
  25.9 3.8 all-to-all-start.2
  29.7 4.3 broadcast.142
  34.0 10.6 %scatter_fusion = bf16[32,128,1024]{2,1,0:T(8,128)(2,1)} fusion(bf16[32,128,1024]{2,1,0:T(8,128)(2,1)} %broadcast.142, s32[14]{0:T(128)S(1)} %compare_select_fusion.2, bf16[14,128,1024]{2,1,0:T(8,128)(2,1)} %bitcast.139), kind=kCustom, calls=%fused_computation.5 | custom fusion | bytes 11010104 | tf_op jit(solution)/shard_map/scatter | solution.py:84
  44.6 7.7 %all-to-all-start.1 = ((bf16[32,128,1024]{2,1,0:T(8,128)(2,1)}), bf16[32,128,1024]{2,1,0:T(8,128)(2,1)}, u32[]{:S(2)}, u32[]{:S(2)}) async-start(bf16[32,128,1024]{2,1,0:T(8,128)(2,1)} %scatter_fusion), calls=%async_computation.1 | async-start | bytes 16777216 | tf_op jit(solution)/shard_map/all_to_all | solution.py:87
  52.4 119.4 %all_gather.19 = bf16[1024,256]{1,0:T(8,128)(2,1)S(1)} all-gather(bf16[32,256]{1,0:T(8,128)(2,1)S(1)} %copy-done.16), channel_id=1, replica_groups=mesh['dp'=32,'mp'=4] {'dp'}, dimensions={0}, use_global_device_ids=true | all-gather | bytes 540672 | tf_op jit(solution)/shard_map/all_gather | solution.py:99
  171.8 25.5 %all_gather.20 = bf16[1024,256]{1,0:T(8,128)(2,1)S(1)} all-gather(bf16[32,256]{1,0:T(8,128)(2,1)S(1)} %copy-done.17), channel_id=1, replica_groups=mesh['dp'=32,'mp'=4] {'dp'}, dimensions={0}, use_global_device_ids=true | all-gather | bytes 540672 | tf_op jit(solution)/shard_map/all_gather | solution.py:100
  197.2 22.1 %all_gather.18 = bf16[1024,256]{1,0:T(8,128)(2,1)S(1)} all-gather(bf16[32,256]{1,0:T(8,128)(2,1)S(1)} %copy-done.18), channel_id=1, replica_groups=mesh['dp'=32,'mp'=4] {'dp'}, dimensions={0}, use_global_device_ids=true | all-gather | bytes 540672 | tf_op jit(solution)/shard_map/all_gather | solution.py:98
  219.3 27.3 %all_gather.21 = bf16[256,1024]{0,1:T(8,128)(2,1)} all-gather(bf16[256,32]{0,1:T(8,128)(2,1)S(1)} %copy-done.19), channel_id=1, replica_groups=mesh['dp'=32,'mp'=4] {'dp'}, dimensions={1}, use_global_device_ids=true | all-gather | bytes 540672 | tf_op jit(solution)/shard_map/all_gather | solution.py:102
  246.7 1.6 clamp_reduce_fusion
  249.0 6.1 gather_fusion
  255.1 3.2 convolution_convert_fusion.3
  260.3 3.2 convolution_convert_fusion.2
  265.4 3.2 convolution_convert_fusion.4
  269.7 7.8 %while.40 = (s32[]{:T(128)}, bf16[2,896,64]{1,2,0:T(8,128)(2,1)S(1)}, s32[2,896]{1,0:T(2,128)S(1)}, s32[14,128]{1,0:T(8,128)S(1)}, bf16[2,896,64]{2,1,0:T(8,128)...) while((s32[]{:T(128)}, bf16[2,896,64]{1,2,0:T(8,128)(2,1)S(1)}, ...), condition=%wide.region_8.9_spmd, body=%wide.region_5.8_spmd.sunk | while | flops 425548032 | bytes 20567648 | solution.py:33
  272.2 1.5 fusion.144
  276.0 1.5 fusion.144
  279.1 7.7 %while.41 = (s32[]{:T(128)}, bf16[2,896,64]{1,2,0:T(8,128)(2,1)S(1)}, s32[2,896]{1,0:T(2,128)S(1)}, s32[14,128]{1,0:T(8,128)S(1)}, bf16[2,896,64]{2,1,0:T(8,128)...) while((s32[]{:T(128)}, bf16[2,896,64]{1,2,0:T(8,128)(2,1)S(1)}, ...), condition=%wide.region_12.13_spmd, body=%wide.region_9.12_spmd.sunk | while | flops 425548032 | bytes 20567648 | solution.py:33
  279.2 1.2 fusion.147
  281.4 1.5 fusion.149
  283.0 1.2 fusion.147
  285.2 1.5 fusion.149
  287.7 7.7 %while.42 = (s32[]{:T(128)}, bf16[2,896,64]{1,2,0:T(8,128)(2,1)S(1)}, s32[2,896]{1,0:T(2,128)S(1)}, s32[14,128]{1,0:T(8,128)S(1)}, bf16[2,896,64]{2,1,0:T(8,128)...) while((s32[]{:T(128)}, bf16[2,896,64]{1,2,0:T(8,128)(2,1)S(1)}, ...), condition=%wide.region_16.17_spmd, body=%wide.region_13.16_spmd.sunk | while | flops 425548032 | bytes 20567648 | solution.py:33
  287.7 1.2 fusion.152
  290.0 1.5 fusion.154
  291.6 1.2 fusion.152
  293.8 1.5 fusion.154
  296.3 7.9 %while.43 = (s32[]{:T(128)}, bf16[2,896,64]{1,2,0:T(8,128)(2,1)S(1)}, s32[2,896]{1,0:T(2,128)S(1)}, s32[14,128]{1,0:T(8,128)S(1)}, bf16[2,896,64]{2,1,0:T(8,128)...) while((s32[]{:T(128)}, bf16[2,896,64]{1,2,0:T(8,128)(2,1)S(1)}, ...), condition=%wide.region_20.21_spmd, body=%wide.region_17.20_spmd.sunk | while | flops 425548032 | bytes 20567648 | solution.py:33
  298.8 1.5 fusion.159
  302.6 1.5 fusion.159
  304.2 3.0 convolution_convert_fusion
  308.5 81.5 %all-reduce.3.cloned.1.call-done = bf16[1792,1024]{1,0:T(8,128)(2,1)} async-done(((bf16[1792,1024]{1,0:T(8,128)(2,1)}), bf16[1792,1024]{1,0:T(8,128)(2,1)}) %all-reduce.3.cloned.1.call-update) | async-done | bytes 3670032 | tf_op jit(solution)/shard_map/psum | solution.py:39
  390.0 4.3 fusion.43
  395.5 2.3 multiply_reduce_fusion.1
  397.8 3.3 add_convert_fusion.1
  401.1 26.1 %convolution_convert_fusion.1 = bf16[1792,1024]{1,0:T(8,128)(2,1)} fusion(bf16[1024,1024]{0,1:T(8,128)(2,1)} %all-gather.5.cloned.1.call-done, bf16[1792,1024]{1,0:T(8,128)(2,1)} %add_convert_fusion.1, bf16[1024,1024]{1,0:T(8,128)(2,1)} %all-gather.3.cloned.1.call-done), kind=kOutput, calls=%fused_computation.86 | convolution fusion | flops 7637303296 | bytes 11534336 | tf_op jit(solution)/shard_map/dot_general | solution.py:126
  428.0 83.4 %all-reduce.5.cloned.1.call-done = bf16[1792,1024]{1,0:T(8,128)(2,1)} async-done(((bf16[1792,1024]{1,0:T(8,128)(2,1)}), bf16[1792,1024]{1,0:T(8,128)(2,1)}) %all-reduce.5.cloned.1.call-update) | async-done | bytes 3670032 | tf_op jit(solution)/shard_map/psum | solution.py:39
  511.4 4.3 fusion.45
  516.7 2.4 multiply_reduce_fusion
  519.2 3.3 add_convert_fusion
  522.5 6.9 %gather_fusion.2 = bf16[32,128,1024]{2,1,0:T(8,128)(2,1)} fusion(bf16[14,128,1024]{2,1,0:T(8,128)(2,1)} %bitcast.136, s32[1024]{0:T(1024)S(1)} %pad_clamp_fusion.1), kind=kCustom, calls=%fused_computation.2 | custom fusion | bytes 16777344 | tf_op jit(solution)/shard_map/gather | solution.py:44
  529.5 7.2 %broadcast_select_fusion = bf16[32,128,1024]{2,1,0:T(8,128)(2,1)} fusion(bf16[32,128,1024]{2,1,0:T(8,128)(2,1)} %gather_fusion.2, pred[32]{0:T(512)(128)(4,1)S(1)} %compare_reduce_fusion), kind=kLoop, calls=%fused_computation.56 | loop fusion | flops 4194304 | bytes 16777248 | tf_op jit(solution)/shard_map/jit(_where)/select_n | solution.py:45
  536.7 7.5 %all-to-all-start.3 = ((bf16[32,128,1024]{2,1,0:T(8,128)(2,1)}), bf16[32,128,1024]{2,1,0:T(8,128)(2,1)}, u32[]{:S(2)}, u32[]{:S(2)}) async-start(bf16[32,128,1024]{2,1,0:T(8,128)(2,1)} %broadcast_select_fusion), calls=%async_computation.3 | async-start | bytes 16777216 | tf_op jit(solution)/shard_map/all_to_all | solution.py:131
  544.3 1.4 pad_maximum_fusion
  545.6 3.6 copy.98
  549.2 100.9 %all-to-all-done.3 = bf16[32,128,1024]{2,1,0:T(8,128)(2,1)} async-done(((bf16[32,128,1024]{2,1,0:T(8,128)(2,1)}), bf16[32,128,1024]{2,1,0:T(8,128)(2,1)}, u32[]{:S(2)}, u32[]{:S(2)}) %all-to-all-start.3) | async-done | bytes 8388640 | tf_op jit(solution)/shard_map/all_to_all | solution.py:131
  650.1 6.0 gather_fusion.3
  (128 shorter events, 29.7 us)
Async XLA Ops:
  8.0 10.6 %copy-start = (s32[1792]{0:T(1024)S(1)}, s32[1792]{0:T(1024)}, u32[]{:S(2)}) copy-start(s32[1792]{0:T(1024)} %param.22) | copy-start | bytes 21508
  8.8 35.8 %copy-start.24 = (s32[14]{0:T(128)}, s32[14]{0:T(128)S(1)}, u32[]{:S(2)}) copy-start(s32[14]{0:T(128)S(1)} %compare_select_fusion.2) | copy-start | bytes 172
  10.1 15.8 %all-to-all-start = ((s32[32,1,1]{2,1,0:T(1,128)}), s32[32,1,1]{2,1,0:T(1,128)S(1)}, u32[]{:S(2)}, u32[]{:S(2)}) async-start(s32[32,1,1]{2,1,0:T(1,128)} %copy.81), calls=%async_computation | async-start | bytes 32768 | tf_op jit(solution)/shard_map/all_to_all | solution.py:89
  25.9 220.8 %copy-start.14 = (s32[32,1,1]{2,1,0:T(1,128)}, s32[32,1,1]{2,1,0:T(1,128)S(1)}, u32[]{:S(2)}) copy-start(s32[32,1,1]{2,1,0:T(1,128)S(1)} %all-to-all-done) | copy-start | bytes 388
  25.9 18.8 %all-to-all-start.2 = ((s32[32,1,128]{2,1,0:T(1,128)}), s32[32,1,128]{2,1,0:T(1,128)S(1)}, u32[]{:S(2)}, u32[]{:S(2)}) async-start(s32[32,1,128]{2,1,0:T(1,128)} %bitcast.18), calls=%async_computation.2 | async-start | bytes 32768 | tf_op jit(solution)/shard_map/all_to_all | solution.py:88
  44.6 7.8 %copy-start.16 = (bf16[32,256]{1,0:T(8,128)(2,1)S(1)}, bf16[32,256]{1,0:T(8,128)(2,1)}, u32[]{:S(2)}) copy-start(bf16[32,256]{1,0:T(8,128)(2,1)} %param.25) | copy-start | bytes 49156
  44.6 127.1 %copy-start.17 = (bf16[32,256]{1,0:T(8,128)(2,1)S(1)}, bf16[32,256]{1,0:T(8,128)(2,1)}, u32[]{:S(2)}) copy-start(bf16[32,256]{1,0:T(8,128)(2,1)} %param.26) | copy-start | bytes 49156
  44.6 152.6 %copy-start.18 = (bf16[32,256]{1,0:T(8,128)(2,1)S(1)}, bf16[32,256]{1,0:T(8,128)(2,1)}, u32[]{:S(2)}) copy-start(bf16[32,256]{1,0:T(8,128)(2,1)} %param.24) | copy-start | bytes 49156
  44.6 174.7 %copy-start.19 = (bf16[256,32]{0,1:T(8,128)(2,1)S(1)}, bf16[256,32]{0,1:T(8,128)(2,1)}, u32[]{:S(2)}) copy-start(bf16[256,32]{0,1:T(8,128)(2,1)} %param.27) | copy-start | bytes 49156
  44.6 204.4 %all-to-all-start.1 = ((bf16[32,128,1024]{2,1,0:T(8,128)(2,1)}), bf16[32,128,1024]{2,1,0:T(8,128)(2,1)}, u32[]{:S(2)}, u32[]{:S(2)}) async-start(bf16[32,128,1024]{2,1,0:T(8,128)(2,1)} %scatter_fusion), calls=%async_computation.1 | async-start | bytes 16777216 | tf_op jit(solution)/shard_map/all_to_all | solution.py:87
  52.3 337.7 %all-reduce.3.cloned.1.call-start = ((), (), s32[]{:S(2)}) async-start(), calls=%async_computation.4 | async-start | bytes 7340032 | tf_op jit(solution)/shard_map/psum | solution.py:39
  258.3 0.9 copy-start.6
  263.5 0.9 copy-start.8
  287.7 7.7 %copy-start.9 = (bf16[1792,64]{0,1:T(8,128)(2,1)S(1)}, bf16[1792,64]{0,1:T(8,128)(2,1)}, u32[]{:S(2)}) copy-start(bf16[1792,64]{0,1:T(8,128)(2,1)} %get-tuple-element.375) | copy-start | bytes 688132
  287.7 8.0 %copy-start.10 = (bf16[1792,64]{0,1:T(8,128)(2,1)S(1)}, bf16[1792,64]{0,1:T(8,128)(2,1)}, u32[]{:S(2)}) copy-start(bf16[1792,64]{0,1:T(8,128)(2,1)} %get-tuple-element.371) | copy-start | bytes 688132
  287.7 8.3 %copy-start.11 = (bf16[1792,64]{0,1:T(8,128)(2,1)S(1)}, bf16[1792,64]{0,1:T(8,128)(2,1)}, u32[]{:S(2)}) copy-start(bf16[1792,64]{0,1:T(8,128)(2,1)} %get-tuple-element.379) | copy-start | bytes 688132
  296.3 7.9 %copy-start.12 = (bf16[256,1024]{0,1:T(8,128)(2,1)S(1)}, bf16[256,1024]{0,1:T(8,128)(2,1)}, u32[]{:S(2)}) copy-start(bf16[256,1024]{0,1:T(8,128)(2,1)} %all_gather.21) | copy-start | bytes 1572868
  296.3 7.9 %copy-start.13 = (bf16[2,8,8,896]{3,2,0,1:T(8,128)(2,1)S(1)}, bf16[2,8,8,896]{3,2,0,1:T(8,128)(2,1)}, u32[]{:S(2)}) copy-start(bf16[2,8,8,896]{3,2,0,1:T(8,128)(2,1)} %copy.103) | copy-start | bytes 688132
  307.3 93.9 %all-gather.3.cloned.1.call-start = ((), (), s32[]{:S(2)}) async-start(), calls=%async_computation.5 | async-start | bytes 2162688 | tf_op jit(solution)/shard_map/all_gather | solution.py:101
  307.8 93.3 %all-gather.5.cloned.1.call-start = ((), (), s32[]{:S(2)}) async-start(), calls=%async_computation.6 | async-start | bytes 2162688 | tf_op jit(solution)/shard_map/all_gather | solution.py:103
  308.4 89.3 %copy-start.20 = (f32[1024]{0:T(1024)S(1)}, f32[1024]{0:T(1024)}, u32[]{:S(2)}) copy-start(f32[1024]{0:T(1024)} %param.31) | copy-start | bytes 12292
  308.4 89.3 %copy-start.21 = (f32[1024]{0:T(1024)S(1)}, f32[1024]{0:T(1024)}, u32[]{:S(2)}) copy-start(f32[1024]{0:T(1024)} %param.30) | copy-start | bytes 12292
  308.5 203.0 %all-reduce.5.cloned.1.call-start = ((), (), s32[]{:S(2)}) async-start(), calls=%async_computation.7 | async-start | bytes 7340032 | tf_op jit(solution)/shard_map/psum | solution.py:39
  390.0 4.4 copy-start.2
  390.0 5.5 copy-start.4
  401.1 26.1 %copy-start.26 = (s32[32]{0:T(128)S(1)}, s32[32]{0:T(128)}, u32[]{:S(2)}) copy-start(s32[32]{0:T(128)} %get-tuple-element.304) | copy-start | bytes 388
  401.1 26.2 %copy-start.15 = (s32[32,1,1]{2,1,0:T(1,128)S(1)}, s32[32,1,1]{2,1,0:T(1,128)}, u32[]{:S(2)}) copy-start(s32[32,1,1]{2,1,0:T(1,128)} %copy-done.14) | copy-start | bytes 388
  428.0 91.2 %copy-start.22 = (f32[1024]{0:T(1024)S(1)}, f32[1024]{0:T(1024)}, u32[]{:S(2)}) copy-start(f32[1024]{0:T(1024)} %param.33) | copy-start | bytes 12292
  428.0 91.2 %copy-start.23 = (f32[1024]{0:T(1024)S(1)}, f32[1024]{0:T(1024)}, u32[]{:S(2)}) copy-start(f32[1024]{0:T(1024)} %param.32) | copy-start | bytes 12292
  511.4 4.3 copy-start.3
  511.4 5.3 copy-start.5
  536.7 7.5 %copy-start.25 = (s32[14]{0:T(128)S(1)}, s32[14]{0:T(128)}, u32[]{:S(2)}) copy-start(s32[14]{0:T(128)} %copy-done.24) | copy-start | bytes 172
  536.7 7.6 %copy-start.7 = (bf16[1792,256]{0,1:T(8,128)(2,1)S(1)}, bf16[1792,256]{0,1:T(8,128)(2,1)}, u32[]{:S(2)}) copy-start(bf16[1792,256]{0,1:T(8,128)(2,1)} %copy-done.6) | copy-start | bytes 2752516
  536.7 113.4 %all-to-all-start.3 = ((bf16[32,128,1024]{2,1,0:T(8,128)(2,1)}), bf16[32,128,1024]{2,1,0:T(8,128)(2,1)}, u32[]{:S(2)}, u32[]{:S(2)}) async-start(bf16[32,128,1024]{2,1,0:T(8,128)(2,1)} %broadcast_select_fusion), calls=%async_computation.3 | async-start | bytes 16777216 | tf_op jit(solution)/shard_map/all_to_all | solution.py:131
  544.3 111.9 %copy-start.1 = (s32[1792]{0:T(1024)S(1)}, s32[1792]{0:T(1024)}, u32[]{:S(2)}) copy-start(s32[1792]{0:T(1024)} %param.22) | copy-start | bytes 21508
Sparse Core Ops, SparseCore 0:
  307.4 82.5 all-reduce.2
  427.4 84.0 all-reduce.4
Sparse Core Ops, SparseCore 1:
  310.0 42.0 all-gather.2
  354.2 42.9 all-gather.4
where the time goes:
time: 670 us; the launch traced here: 664 us
  waiting for transfers between devices  273 us (41%)
  blocking collectives  194 us (29%)
  matrix products  60.8 us (9%)
  local copies, waits for them, and re-layouts  51.1 us (8%)
  other arithmetic  40.1 us (6%)
  starting transfers between devices  27.6 us (4%)
  between operations  16.2 us (2%)
    psum x2, waiting for transfers between devices, finish(): lax.psum(partial_value.astype(jnp.bfloat16), 'mp').astype(jnp.float32)  165 us
    all_gather x1, blocking collectives, body(): lax.all_gather(w_key, 'dp', axis=0, tiled=True)  119 us
    all_to_all x1, waiting for transfers between devices, body(): lax.all_to_all(outgoing_pages(second, got_slots, pages_dev, page), 'dp',...  101 us
    all_gather x1, blocking collectives, body(): lax.all_gather(w_out, 'dp', axis=1, tiled=True)  27.3 us
    dot_general x1, matrix products, body(): jnp.dot(hidden, full_down, preferred_element_type=jnp.float32)  26.1 us
    all_gather x1, blocking collectives, body(): lax.all_gather(w_value, 'dp', axis=0, tiled=True)  25.5 us
    all_gather x1, blocking collectives, body(): lax.all_gather(w_query, 'dp', axis=0, tiled=True)  22.1 us
  transfers between devices with their start and end apart: 8, of which 4 were waited for; matrix products, arithmetic and copies ran while one was open for 5% of the time, Pallas kernels for 0%

commit v1 on v0

--- a/solution.py
+++ b/solution.py
@@ -36,7 +36,11 @@
 
 
 def finish(partial_value, residual, gain, shift):
-    total = lax.psum(partial_value.astype(jnp.bfloat16), "mp").astype(jnp.float32)
+    total = (
+        jax.lax.all_gather(partial_value.astype(jnp.bfloat16), axis_name="mp")
+        .sum(axis=0)
+        .astype(jnp.float32)
+    )
     return layer_norm(residual.astype(jnp.float32) + total, gain, shift).astype(jnp.bfloat16)
 
 

time: 670 us -> 871 us (1.30)
  waiting for transfers between devices: 273 us -> 447 us
  other arithmetic: 40.1 us -> 70.1 us
    all_gather x0 -> x2, waiting for transfers between devices: none -> 268 us  [finish(): jax.lax.all_gather(partial_value.astype(jnp.bfloat16), axis_name='mp')]
    psum x2 -> x0, waiting for transfers between devices: 165 us -> none  [finish(): lax.psum(partial_value.astype(jnp.bfloat16), 'mp').astype(jnp.float32)]
    all_gather x1, blocking collectives: 22.1 us -> 119 us  [body(): lax.all_gather(w_query, 'dp', axis=0, tiled=True)]
    all_gather x1, blocking collectives: 119 us -> 25.5 us  [body(): lax.all_gather(w_key, 'dp', axis=0, tiled=True)]
    all_gather x1, waiting for transfers between devices: 0.01 us -> 45.3 us  [body(): lax.all_gather(w_down, 'dp', axis=1, tiled=True)]
    all_gather x1, waiting for transfers between devices: 0.01 us -> 24.9 us  [body(): lax.all_gather(w_up, 'dp', axis=0, tiled=True)]
    reduce_sum x0 -> x2, other arithmetic: none -> 22.3 us  [finish(): total = jax.lax.all_gather(partial_value.astype(jnp.bfloat16), axis_name=...]
  transfers between devices with their start and end apart: 8 -> 8, of which waited for: 4 -> 6; matrix products, arithmetic and copies ran while one was open for 5% -> 5% of each run, Pallas kernels for 0% -> 0%
where the time goes in v1:
time: 871 us; the launch traced here: 864 us
  waiting for transfers between devices  447 us (51%)
  blocking collectives  194 us (22%)
  other arithmetic  70.1 us (8%)
  matrix products  59.2 us (7%)
  local copies, waits for them, and re-layouts  51.1 us (6%)
  starting transfers between devices  27.6 us (3%)
  between operations  14.5 us (2%)
    all_gather x2, waiting for transfers between devices, finish(): jax.lax.all_gather(partial_value.astype(jnp.bfloat16), axis_name='mp')  268 us
    all_gather x1, blocking collectives, body(): lax.all_gather(w_query, 'dp', axis=0, tiled=True)  119 us
    all_to_all x1, waiting for transfers between devices, body(): lax.all_to_all(outgoing_pages(second, got_slots, pages_dev, page), 'dp',...  101 us
    all_gather x1, waiting for transfers between devices, body(): lax.all_gather(w_down, 'dp', axis=1, tiled=True)  45.3 us
    all_gather x1, blocking collectives, body(): lax.all_gather(w_out, 'dp', axis=1, tiled=True)  27.3 us
    dot_general x1, matrix products, body(): jnp.dot(hidden, full_down, preferred_element_type=jnp.float32)  26.1 us
    all_gather x1, blocking collectives, body(): lax.all_gather(w_key, 'dp', axis=0, tiled=True)  25.5 us
    all_gather x1, waiting for transfers between devices, body(): lax.all_gather(w_up, 'dp', axis=0, tiled=True)  24.9 us
  transfers between devices with their start and end apart: 8, of which 6 were waited for; matrix products, arithmetic and copies ran while one was open for 5% of the time, Pallas kernels for 0%

profile of v1, /device:TPU:0, one launch (start us, length us, event | category | flops | bytes accessed | tf_op | source)
XLA Modules:
  0.0 864.2 jit_solution(7369539744846020982)
XLA Ops:
  9.3 8.4 all-to-all-start
  18.9 6.1 all-to-all-done
  25.0 3.8 all-to-all-start.2
  28.9 4.3 broadcast.272
  33.2 10.6 %scatter_fusion = bf16[32,128,1024]{2,1,0:T(8,128)(2,1)} fusion(bf16[32,128,1024]{2,1,0:T(8,128)(2,1)} %broadcast.272, s32[14]{0:T(128)S(1)} %compare_select_fusion.2, bf16[14,128,1024]{2,1,0:T(8,128)(2,1)} %bitcast.158), kind=kCustom, calls=%fused_computation.5 | custom fusion | bytes 11010104 | tf_op jit(solution)/shard_map/scatter | solution.py:88
  43.8 7.7 all-to-all-start.1
  51.5 119.4 %all_gather.30 = bf16[1024,256]{1,0:T(8,128)(2,1)S(1)} all-gather(bf16[32,256]{1,0:T(8,128)(2,1)S(1)} %copy-done.22), channel_id=1, replica_groups=mesh['dp'=32,'mp'=4] {'dp'}, dimensions={0}, use_global_device_ids=true | all-gather | bytes 540672 | tf_op jit(solution)/shard_map/all_gather | solution.py:102
  170.9 25.5 %all_gather.31 = bf16[1024,256]{1,0:T(8,128)(2,1)S(1)} all-gather(bf16[32,256]{1,0:T(8,128)(2,1)S(1)} %copy-done.23), channel_id=1, replica_groups=mesh['dp'=32,'mp'=4] {'dp'}, dimensions={0}, use_global_device_ids=true | all-gather | bytes 540672 | tf_op jit(solution)/shard_map/all_gather | solution.py:103
  196.4 22.1 %all_gather.32 = bf16[1024,256]{1,0:T(8,128)(2,1)S(1)} all-gather(bf16[32,256]{1,0:T(8,128)(2,1)S(1)} %copy-done.24), channel_id=1, replica_groups=mesh['dp'=32,'mp'=4] {'dp'}, dimensions={0}, use_global_device_ids=true | all-gather | bytes 540672 | tf_op jit(solution)/shard_map/all_gather | solution.py:104
  218.5 27.3 %all_gather.33 = bf16[256,1024]{0,1:T(8,128)(2,1)} all-gather(bf16[256,32]{0,1:T(8,128)(2,1)S(1)} %copy-done.25), channel_id=1, replica_groups=mesh['dp'=32,'mp'=4] {'dp'}, dimensions={1}, use_global_device_ids=true | all-gather | bytes 540672 | tf_op jit(solution)/shard_map/all_gather | solution.py:106
  245.8 1.6 clamp_reduce_fusion
  248.2 6.1 gather_fusion
  254.2 3.4 convolution_convert_fusion.2
  267.8 10.2 %while.40 = (s32[]{:T(128)}, bf16[2,896,64]{1,2,0:T(8,128)(2,1)S(1)}, s32[2,896]{1,0:T(2,128)S(1)}, s32[14,128]{1,0:T(8,128)S(1)}, bf16[2,896,64]{2,1,0:T(8,128)...) while((s32[]{:T(128)}, bf16[2,896,64]{1,2,0:T(8,128)(2,1)S(1)}, ...), condition=%wide.region_8.9_spmd, body=%wide.region_5.8_spmd.sunk | while | flops 425548032 | bytes 20566120 | solution.py:33
  268.0 2.4 fusion.143
  271.4 1.5 fusion.145
  273.0 2.4 fusion.143
  276.4 1.5 fusion.145
  278.9 7.7 while.43
  281.2 1.5 fusion.160
  285.1 1.5 fusion.160
  287.0 7.7 while.42
  289.3 1.5 fusion.155
  293.1 1.5 fusion.155
  295.0 7.9 while.41
  297.5 1.5 fusion.150
  301.4 1.5 fusion.150
  303.0 3.0 convolution_convert_fusion
  307.5 133.3 %all-gather.11.cloned.1.call-done = bf16[7168,1024]{1,0:T(8,128)(2,1)} async-done(((bf16[1792,1024]{1,0:T(8,128)(2,1)}), bf16[7168,1024]{1,0:T(8,128)(2,1)}) %all-gather.11.cloned.1.call-update) | async-done | bytes 14680080 | tf_op jit(solution)/shard_map/all_gather | solution.py:40
  440.8 11.0 %reduce_sum.119 = bf16[1792,1024]{1,0:T(8,128)(2,1)} reduce(bf16[4,1792,1024]{2,1,0:T(8,128)(2,1)} %bitcast.154, bf16[]{:T(256)} %constant.100.clone.1), dimensions={0}, to_apply=%region_21.22 | reduce | flops 5505024 | bytes 18350082 | tf_op jit(solution)/shard_map/reduce_sum | solution.py:41
  451.8 4.4 fusion.44
  457.2 2.3 multiply_reduce_fusion.1
  459.5 3.4 add_convert_fusion.1
  462.9 24.9 %all-gather.7.cloned.1.call-done = bf16[1024,1024]{1,0:T(8,128)(2,1)} async-done(((bf16[32,1024]{1,0:T(8,128)(2,1)}), bf16[1024,1024]{1,0:T(8,128)(2,1)}) %all-gather.7.cloned.1.call-update) | async-done | bytes 2097168 | tf_op jit(solution)/shard_map/all_gather | solution.py:105
  487.8 45.3 %all-gather.9.cloned.1.call-done = bf16[1024,1024]{0,1:T(8,128)(2,1)} async-done(((bf16[1024,32]{0,1:T(8,128)(2,1)}), bf16[1024,1024]{0,1:T(8,128)(2,1)}) %all-gather.9.cloned.1.call-update) | async-done | bytes 2097168 | tf_op jit(solution)/shard_map/all_gather | solution.py:107
  533.1 26.1 %convolution_convert_fusion.1 = bf16[1792,1024]{1,0:T(8,128)(2,1)} fusion(bf16[1024,1024]{0,1:T(8,128)(2,1)} %all-gather.9.cloned.1.call-done, bf16[1792,1024]{1,0:T(8,128)(2,1)} %add_convert_fusion.1, bf16[1024,1024]{1,0:T(8,128)(2,1)} %all-gather.7.cloned.1.call-done), kind=kOutput, calls=%fused_computation.84 | convolution fusion | flops 7637303296 | bytes 11534336 | tf_op jit(solution)/shard_map/dot_general | solution.py:130
  559.9 135.0 %all-gather.13.cloned.1.call-done = bf16[7168,1024]{1,0:T(8,128)(2,1)} async-done(((bf16[1792,1024]{1,0:T(8,128)(2,1)}), bf16[7168,1024]{1,0:T(8,128)(2,1)}) %all-gather.13.cloned.1.call-update) | async-done | bytes 14680080 | tf_op jit(solution)/shard_map/all_gather | solution.py:40
  694.9 11.3 %reduce_sum.122 = bf16[1792,1024]{1,0:T(8,128)(2,1)} reduce(bf16[4,1792,1024]{2,1,0:T(8,128)(2,1)} %bitcast.155, bf16[]{:T(256)} %constant.100.clone.1), dimensions={0}, to_apply=%region_24.25 | reduce | flops 5505024 | bytes 18350082 | tf_op jit(solution)/shard_map/reduce_sum | solution.py:41
  706.2 4.3 fusion.42
  710.5 5.0 multiply_reduce_fusion
  715.5 8.4 add_convert_fusion
  723.9 6.9 gather_fusion.2
  730.9 7.2 broadcast_select_fusion
  738.1 7.5 all-to-all-start.3
  745.7 1.4 pad_maximum_fusion
  747.0 3.6 copy.98
  750.6 100.9 %all-to-all-done.3 = bf16[32,128,1024]{2,1,0:T(8,128)(2,1)} async-done(((bf16[32,128,1024]{2,1,0:T(8,128)(2,1)}), bf16[32,128,1024]{2,1,0:T(8,128)(2,1)}, u32[]{:S(2)}, u32[]{:S(2)}) %all-to-all-start.3) | async-done | bytes 8388640 | tf_op jit(solution)/shard_map/all_to_all | solution.py:135
  851.5 6.0 gather_fusion.3
  (138 shorter events, 34.8 us)
Async XLA Ops:
  7.2 10.6 %copy-start = (s32[1792]{0:T(1024)S(1)}, s32[1792]{0:T(1024)}, u32[]{:S(2)}) copy-start(s32[1792]{0:T(1024)} %param.22) | copy-start | bytes 21508
  8.0 35.8 %copy-start.28 = (s32[14]{0:T(128)}, s32[14]{0:T(128)S(1)}, u32[]{:S(2)}) copy-start(s32[14]{0:T(128)S(1)} %compare_select_fusion.2) | copy-start | bytes 172
  9.3 15.8 %all-to-all-start = ((s32[32,1,1]{2,1,0:T(1,128)}), s32[32,1,1]{2,1,0:T(1,128)S(1)}, u32[]{:S(2)}, u32[]{:S(2)}) async-start(s32[32,1,1]{2,1,0:T(1,128)} %copy.81), calls=%async_computation | async-start | bytes 32768 | tf_op jit(solution)/shard_map/all_to_all | solution.py:93
  25.0 220.8 %copy-start.18 = (s32[32,1,1]{2,1,0:T(1,128)}, s32[32,1,1]{2,1,0:T(1,128)S(1)}, u32[]{:S(2)}) copy-start(s32[32,1,1]{2,1,0:T(1,128)S(1)} %all-to-all-done) | copy-start | bytes 388
  25.0 18.8 %all-to-all-start.2 = ((s32[32,1,128]{2,1,0:T(1,128)}), s32[32,1,128]{2,1,0:T(1,128)S(1)}, u32[]{:S(2)}, u32[]{:S(2)}) async-start(s32[32,1,128]{2,1,0:T(1,128)} %bitcast.17), calls=%async_computation.2 | async-start | bytes 32768 | tf_op jit(solution)/shard_map/all_to_all | solution.py:92
  43.8 7.8 copy-start.22
  43.8 127.1 %copy-start.23 = (bf16[32,256]{1,0:T(8,128)(2,1)S(1)}, bf16[32,256]{1,0:T(8,128)(2,1)}, u32[]{:S(2)}) copy-start(bf16[32,256]{1,0:T(8,128)(2,1)} %param.25) | copy-start | bytes 49156
  43.8 152.6 %copy-start.24 = (bf16[32,256]{1,0:T(8,128)(2,1)S(1)}, bf16[32,256]{1,0:T(8,128)(2,1)}, u32[]{:S(2)}) copy-start(bf16[32,256]{1,0:T(8,128)(2,1)} %param.26) | copy-start | bytes 49156
  43.8 174.7 %copy-start.25 = (bf16[256,32]{0,1:T(8,128)(2,1)S(1)}, bf16[256,32]{0,1:T(8,128)(2,1)}, u32[]{:S(2)}) copy-start(bf16[256,32]{0,1:T(8,128)(2,1)} %param.27) | copy-start | bytes 49156
  43.8 204.3 %all-to-all-start.1 = ((bf16[32,128,1024]{2,1,0:T(8,128)(2,1)}), bf16[32,128,1024]{2,1,0:T(8,128)(2,1)}, u32[]{:S(2)}, u32[]{:S(2)}) async-start(bf16[32,128,1024]{2,1,0:T(8,128)(2,1)} %scatter_fusion), calls=%async_computation.1 | async-start | bytes 16777216 | tf_op jit(solution)/shard_map/all_to_all | solution.py:91
  51.5 389.3 %all-gather.11.cloned.1.call-start = ((), (), s32[]{:S(2)}) async-start(), calls=%async_computation.6 | async-start | bytes 18350080 | tf_op jit(solution)/shard_map/all_gather | solution.py:40
  254.2 3.4 copy-start.2
  257.6 9.1 %copy-start.8 = (bf16[1792,256]{0,1:T(8,128)(2,1)}, bf16[1792,256]{0,1:T(8,128)(2,1)S(1)}, u32[]{:S(2)}) copy-start(bf16[1792,256]{0,1:T(8,128)(2,1)S(1)} %convolution_convert_fusion.2) | copy-start | bytes 2752516
  258.8 4.5 copy-start.10
  267.7 11.2 %copy-start.15 = (bf16[1792,64]{1,0:T(8,128)(2,1)S(1)}, bf16[1792,64]{1,0:T(8,128)(2,1)}, u32[]{:S(2)}) copy-start(bf16[1792,64]{1,0:T(8,128)(2,1)} %copy.102) | copy-start | bytes 688132
  267.7 11.2 %copy-start.16 = (bf16[1792,64]{1,0:T(8,128)(2,1)S(1)}, bf16[1792,64]{1,0:T(8,128)(2,1)}, u32[]{:S(2)}) copy-start(bf16[1792,64]{1,0:T(8,128)(2,1)} %copy.95) | copy-start | bytes 688132
  287.0 7.7 copy-start.11
  287.0 8.0 copy-start.13
  287.0 8.0 copy-start.14
  295.0 7.9 copy-start.12
  295.0 7.9 copy-start.17
  305.9 181.8 %all-gather.7.cloned.1.call-start = ((), (), s32[]{:S(2)}) async-start(), calls=%async_computation.4 | async-start | bytes 2162688 | tf_op jit(solution)/shard_map/all_gather | solution.py:105
  306.7 226.4 %all-gather.9.cloned.1.call-start = ((), (), s32[]{:S(2)}) async-start(), calls=%async_computation.5 | async-start | bytes 2162688 | tf_op jit(solution)/shard_map/all_gather | solution.py:107
  307.4 387.5 %all-gather.13.cloned.1.call-start = ((), (), s32[]{:S(2)}) async-start(), calls=%async_computation.7 | async-start | bytes 18350080 | tf_op jit(solution)/shard_map/all_gather | solution.py:40
  451.8 4.4 copy-start.3
  451.8 5.4 copy-start.5
  451.8 7.7 copy-start.20
  451.8 7.7 copy-start.21
  462.9 96.4 %copy-start.30 = (s32[32]{0:T(128)S(1)}, s32[32]{0:T(128)}, u32[]{:S(2)}) copy-start(s32[32]{0:T(128)} %get-tuple-element.304) | copy-start | bytes 388
  462.9 96.4 %copy-start.19 = (s32[32,1,1]{2,1,0:T(1,128)S(1)}, s32[32,1,1]{2,1,0:T(1,128)}, u32[]{:S(2)}) copy-start(s32[32,1,1]{2,1,0:T(1,128)} %copy-done.18) | copy-start | bytes 388
  706.2 9.3 %copy-start.4 = (bf16[14,128,1024]{2,1,0:T(8,128)(2,1)S(1)}, bf16[14,128,1024]{2,1,0:T(8,128)(2,1)}, u32[]{:S(2)}) copy-start(bf16[14,128,1024]{2,1,0:T(8,128)(2,1)} %gather_fusion) | copy-start | bytes 11010052
  706.2 9.3 %copy-start.6 = (bf16[1792,1024]{1,0:T(8,128)(2,1)S(1)}, bf16[1792,1024]{1,0:T(8,128)(2,1)}, u32[]{:S(2)}) copy-start(bf16[1792,1024]{1,0:T(8,128)(2,1)} %reduce_sum.119) | copy-start | bytes 11010052
  706.2 9.3 %copy-start.7 = (bf16[1792,1024]{1,0:T(8,128)(2,1)S(1)}, bf16[1792,1024]{1,0:T(8,128)(2,1)}, u32[]{:S(2)}) copy-start(bf16[1792,1024]{1,0:T(8,128)(2,1)} %reduce_sum.122) | copy-start | bytes 11010052
  706.2 9.3 %copy-start.26 = (f32[1024]{0:T(1024)S(1)}, f32[1024]{0:T(1024)}, u32[]{:S(2)}) copy-start(f32[1024]{0:T(1024)} %param.33) | copy-start | bytes 12292
  706.2 9.4 %copy-start.27 = (f32[1024]{0:T(1024)S(1)}, f32[1024]{0:T(1024)}, u32[]{:S(2)}) copy-start(f32[1024]{0:T(1024)} %param.32) | copy-start | bytes 12292
  738.1 7.5 copy-start.29
  738.1 7.6 copy-start.9
  738.1 113.4 %all-to-all-start.3 = ((bf16[32,128,1024]{2,1,0:T(8,128)(2,1)}), bf16[32,128,1024]{2,1,0:T(8,128)(2,1)}, u32[]{:S(2)}, u32[]{:S(2)}) async-start(bf16[32,128,1024]{2,1,0:T(8,128)(2,1)} %broadcast_select_fusion), calls=%async_computation.3 | async-start | bytes 16777216 | tf_op jit(solution)/shard_map/all_to_all | solution.py:135
  745.7 111.9 %copy-start.1 = (s32[1792]{0:T(1024)S(1)}, s32[1792]{0:T(1024)}, u32[]{:S(2)}) copy-start(s32[1792]{0:T(1024)} %param.22) | copy-start | bytes 21508
Sparse Core Ops, SparseCore 0:
  306.1 134.6 all-gather.10
  443.0 44.7 all-gather.6
  490.0 42.9 all-gather.8
  559.4 135.4 all-gather.12
